TPU v7x, 512 devices: a whole 4x4x16 slice. The times are simulated.
512 devices in a mesh: wide: 64 (over x, z), narrow: 8 (over y, core).
Axes of the slice: x: 4, y: 4, z: 16, core: 2. Of those that a mesh axis runs over, the one named last changes fastest.
Arguments:
- tokens: bfloat16 [49152, 2048], P('wide', 'narrow'), may hold values from -6 to 6
- norm_gain: float32 [2048], replicated, may hold values from 0.1 to 1.9
- qkv_weight: bfloat16 [2048, 3, 2048], P('wide', None, 'narrow'), may hold values from -0.125 to 0.125
- out_weight: bfloat16 [2048, 2048], P('wide', 'narrow'), may hold values from -0.25 to 0.25
- cache_pool: bfloat16 [1536, 128, 2, 2048], P('wide', None, None, 'narrow'), may hold values from -400 to 400, as said below
- prefix_pool: bfloat16 [2048, 2, 2048], P('wide', None, 'narrow'), may hold values from -6 to 6
- page_table: int32 [64, 24], P('wide'), may hold values from 0 to 23, each once within a row
- cache_len: int32 [64], P('wide'), may hold values from 512 to 3072
- group_ids: int32 [64], P('wide'), may hold values from 0 to 7, as said below
- group_pages: int32 [16], replicated, may hold values from 0 to 15, each once
Outputs:
- branch_out: bfloat16 [49152, 2048], P('wide', 'narrow')
- new_pages: bfloat16 [49152, 2, 2048], P('wide', None, 'narrow')
Inputs may be any that keep to these rules, and one draw needn't show every extreme that they name: `page_table`: each row is a permutation of the 24 pages of that request. `group_ids`: each group has 8 requests. `group_pages`: a permutation of the prefix pool's pages. `cache_pool`: keys are stored already rotated.
All inputs are finite; a program needn't handle non-finite values.
Results may differ from a plain program's by a relative error of at most 0.0095.
The roundings to bfloat16 on the way count: a program that leaves them out, or rounds other values in their place, can miss the bound.
Values may be sent and summed in bfloat16 or wider, within the bound.
No kernel may reach another device: no remote copies, remote signals or barrier semaphores. Data moves between devices by JAX's collectives and lax.ppermute only.
A program may use at most 128 MiB of HBM per device.

v0:
```python
import jax
import jax.numpy as jnp
from jax import lax
from jax.sharding import Mesh, PartitionSpec as P

HEAD_DIM = 64
ROT = 16
PAGE = 128
KB = 8
PPAGES = 2
NEGATIVE = -1e30


def rotary(vectors, positions):
    half_rot = ROT // 2
    frequency = 10000.0 ** (-(jnp.arange(half_rot, dtype=jnp.float32) * 2.0 / ROT))
    angles = positions.astype(jnp.float32)[:, None] * frequency[None, :]
    cos_part = jnp.concatenate([jnp.cos(angles), jnp.cos(angles)], axis=1)[:, None, :]
    sine_part = jnp.concatenate([jnp.sin(angles), jnp.sin(angles)], axis=1)[:, None, :]
    rotated_in = vectors[..., :ROT]
    turned = jnp.concatenate([-rotated_in[..., half_rot:], rotated_in[..., :half_rot]], axis=-1)
    return jnp.concatenate(
        [rotated_in * cos_part + turned * sine_part, vectors[..., ROT:]], axis=-1
    )


def attend(running, queries, keys, values, key_valid):
    row_max, weight_sum, weighted = running
    scores = jnp.einsum("qhd,khd->hqk", queries, keys, preferred_element_type=jnp.float32) * 0.125
    scores = jnp.where(key_valid[None], scores, NEGATIVE)
    new_max = jnp.maximum(row_max, jnp.max(scores, axis=2))
    expo = jnp.where(key_valid[None], jnp.exp(scores - new_max[:, :, None]), 0.0)
    factor = jnp.exp(row_max - new_max)
    weight_sum = weight_sum * factor + jnp.sum(expo, axis=2)
    update = jnp.einsum(
        "hqk,khd->qhd", expo.astype(jnp.bfloat16), values, preferred_element_type=jnp.float32
    )
    weighted = weighted * jnp.transpose(factor)[:, :, None] + update
    return (new_max, weight_sum, weighted)


def gather_columns(part):
    count = lax.axis_size("narrow")
    copies = jnp.broadcast_to(part[None], (count,) + part.shape)
    received = lax.all_to_all(copies, "narrow", 0, 0, tiled=False)
    return jnp.transpose(received, (1, 0, 2)).reshape(part.shape[0], count * part.shape[1])


def local(
    tokens,
    norm_gain,
    qkv_weight,
    out_weight,
    cache_pool,
    prefix_pool,
    page_table,
    cache_len,
    group_ids,
    group_pages,
):
    span_rows = tokens.shape[0]
    local_width = qkv_weight.shape[2]
    heads_here = local_width // HEAD_DIM
    gathered = gather_columns(tokens)
    widened = gathered.astype(jnp.float32)
    row_mean = jnp.mean(widened, axis=1, keepdims=True)
    centered = widened - row_mean
    variance = jnp.mean(centered * centered, axis=1, keepdims=True)
    normed = (centered * lax.rsqrt(variance + 1e-05) * norm_gain).astype(jnp.bfloat16)
    shard_rows = qkv_weight.shape[0]
    merged = jnp.concatenate(
        [
            qkv_weight.reshape(shard_rows, 3 * local_width),
            out_weight,
            prefix_pool.reshape(shard_rows, 2 * local_width),
        ],
        axis=1,
    )
    along_x = lax.axis_size("wx")
    by_x = lax.all_to_all(
        jnp.broadcast_to(merged[None], (along_x,) + merged.shape), "wx", 0, 0, tiled=False
    )
    by_xz = lax.all_gather(by_x, "wz", axis=0, tiled=False)
    merged_whole = jnp.transpose(by_xz, (1, 0, 2, 3)).reshape(-1, merged.shape[1])
    piece_rows = merged_whole[:, : 3 * local_width]
    out_rows = merged_whole[:, 3 * local_width : 4 * local_width]
    prefix_whole = merged_whole[:, 4 * local_width :]
    piece_count = piece_rows.shape[0]
    columns = normed
    projected = jnp.dot(
        columns,
        piece_rows.reshape(piece_count, 3 * local_width),
        preferred_element_type=jnp.float32,
    )
    projected = projected.reshape(span_rows, 3, heads_here, HEAD_DIM)
    length = cache_len[0]
    offset = jnp.arange(span_rows, dtype=jnp.int32)
    positions = PPAGES * PAGE + length + offset
    queries = rotary(projected[:, 0], positions).astype(jnp.bfloat16)
    keys = rotary(projected[:, 1], positions).astype(jnp.bfloat16)
    values = projected[:, 2].astype(jnp.bfloat16)
    new_pages = jnp.stack(
        [keys.reshape(span_rows, local_width), values.reshape(span_rows, local_width)], axis=1
    )
    initial = (
        jnp.full((heads_here, span_rows), NEGATIVE, jnp.float32),
        jnp.zeros((heads_here, span_rows), jnp.float32),
        jnp.zeros((span_rows, heads_here, HEAD_DIM), jnp.float32),
    )
    running = attend(initial, queries, keys, values, offset[:, None] >= offset[None, :])
    my_group = group_ids[0]
    chosen = lax.dynamic_slice_in_dim(group_pages, my_group * PPAGES, PPAGES)
    key_rows = jnp.concatenate(
        [
            lax.dynamic_slice_in_dim(prefix_whole, chosen[k] * PAGE, PAGE, axis=0)
            for k in range(PPAGES)
        ],
        axis=0,
    ).reshape(PPAGES * PAGE, 2, heads_here, HEAD_DIM)
    running = attend(
        running,
        queries,
        key_rows[:, 0],
        key_rows[:, 1],
        jnp.ones((span_rows, PPAGES * PAGE), dtype=bool),
    )
    page_list = page_table[0]
    page_count = cache_pool.shape[0]
    slot_of_page = (
        jnp.zeros((page_count,), jnp.int32)
        .at[page_list]
        .set(jnp.arange(page_count, dtype=jnp.int32))
    )
    block_keys = KB * PAGE
    key_offset = jnp.arange(block_keys, dtype=jnp.int32)

    def cache_block(block_index, state_now):
        key_rows = lax.dynamic_slice_in_dim(cache_pool, block_index * KB, KB, axis=0).reshape(
            block_keys, 2, heads_here, HEAD_DIM
        )
        slots = lax.dynamic_slice_in_dim(slot_of_page, block_index * KB, KB)
        key_slot = jnp.repeat(slots, PAGE) * PAGE + key_offset % PAGE
        key_valid = jnp.broadcast_to((key_slot < length)[None, :], (span_rows, block_keys))
        return attend(state_now, queries, key_rows[:, 0], key_rows[:, 1], key_valid)

    running = lax.fori_loop(0, page_count // KB, cache_block, running)
    head_values = (
        (running[2] / jnp.transpose(running[1])[:, :, None])
        .astype(jnp.bfloat16)
        .reshape(span_rows, local_width)
    )
    all_heads = lax.all_gather(head_values, "narrow", axis=1, tiled=True)
    columns = all_heads
    branch_out = jnp.dot(columns, out_rows, preferred_element_type=jnp.float32)
    return (branch_out.astype(jnp.bfloat16), new_pages)


def split_mesh(mesh):
    grid = mesh.devices
    try:
        along_x = len({device.coords[0] for device in grid[:, 0]})
    except (AttributeError, TypeError):
        along_x = 4
    shape = (along_x, grid.shape[0] // along_x, grid.shape[1])
    return Mesh(grid.reshape(shape), ("wx", "wz", "narrow"))


def solution(mesh):
    W = ("wx", "wz")
    placed = (
        P(W, "narrow"),
        P(),
        P(W, None, "narrow"),
        P(W, "narrow"),
        P(W, None, None, "narrow"),
        P(W, None, "narrow"),
        P(W, None),
        P(W),
        P(W),
        P(),
    )
    return jax.shard_map(
        local,
        mesh=split_mesh(mesh),
        in_specs=placed,
        out_specs=(P(W, "narrow"), P(W, None, "narrow")),
        check_vma=False,
    )
```

profile of v0, /device:TPU:1, one launch (start us, length us, event | category | flops | bytes accessed | tf_op | source)
XLA Modules:
  0.0 230.6 jit_solution(7096636370363122591)
XLA Ops:
  7.2 0.8 copy.57
  8.0 0.8 copy.56
  8.8 0.7 pad_maximum_fusion.3
  9.6 11.0 %all_to_all.10 = bf16[4,32,1536]{2,1,0:T(8,128)(2,1)} all-to-all(bf16[4,32,1536]{2,1,0:T(8,128)(2,1)S(1)} %broadcast_in_dim.158), channel_id=1, replica_groups=mesh['wx'=4,'wz'=16,'narrow'=8] {'wx'}, dimensions={0} | all-to-all | bytes 786432 | tf_op jit(solution)/shard_map/all_to_all | solution.py:80
  20.6 2.8 %broadcast_in_dim.157 = bf16[8,768,256]{2,1,0:T(8,128)(2,1)} broadcast(bf16[768,256]{1,0:T(8,128)(2,1)} %param.12), dimensions={1,2} | broadcast | bytes 3538944 | tf_op jit(solution)/shard_map/broadcast_in_dim | solution.py:44
  23.4 10.7 %all-to-all-start = ((bf16[8,768,256]{2,1,0:T(8,128)(2,1)}), bf16[8,768,256]{2,1,0:T(8,128)(2,1)}, u32[]{:S(2)}, u32[]{:S(2)}) async-start(bf16[8,768,256]{2,1,0:T(8,128)(2,1)} %broadcast_in_dim.157), calls=%async_computation | async-start | bytes 6291456 | tf_op jit(solution)/shard_map/all_to_all | solution.py:45
  34.8 0.6 fusion.78
  37.4 0.6 scatter_custom_fusion
  38.1 0.2 multiply_cosine_fusion
  38.3 0.7 pad_maximum_fusion.4
  38.9 1.0 iota_compare_fusion
  39.9 31.7 %all-to-all-done = bf16[8,768,256]{2,1,0:T(8,128)(2,1)} async-done(((bf16[8,768,256]{2,1,0:T(8,128)(2,1)}), bf16[8,768,256]{2,1,0:T(8,128)(2,1)}, u32[]{:S(2)}, u32[]{:S(2)}) %all-to-all-start) | async-done | bytes 3145760 | tf_op jit(solution)/shard_map/all_to_all | solution.py:45
  71.6 3.2 %copy.39 = bf16[8,768,256]{1,2,0:T(8,128)(2,1)S(1)} copy(bf16[8,768,256]{2,1,0:T(8,128)(2,1)} %all-to-all-done) | data formatting | bytes 6291456 | tf_op jit(solution)/shard_map/all_to_all | solution.py:45
  74.8 0.5 convert_reduce_fusion
  75.4 0.9 fusion.33
  76.2 2.6 %fusion.35 = bf16[8,768,256]{1,2,0:T(8,128)(2,1)} fusion(bf16[8,768,256]{1,2,0:T(8,128)(2,1)S(1)} %copy.39, f32[8,256]{1,0:T(8,128)S(1)} %mul.207, f32[768]{0:T(1024)S(1)} %add_rsqrt_fusion, f32[768]{0:T(1024)S(1)} %broadcast_multiply_fusion), kind=kLoop, calls=%fused_computation.44 | loop fusion | flops 7864320 | bytes 6305792 | tf_op jit(solution)/shard_map/convert.3
  78.9 29.6 %all-gather.6.cloned.1.call-done = bf16[64,32,1536]{2,1,0:T(8,128)(2,1)} async-done(((bf16[4,32,1536]{2,1,0:T(8,128)(2,1)}), bf16[64,32,1536]{2,1,0:T(8,128)(2,1)}) %all-gather.6.cloned.1.call-update) | async-done | bytes 6291472 | tf_op jit(solution)/shard_map/all_gather | solution.py:83
  108.5 3.5 %copy.41 = bf16[4,16,32,1536]{3,2,1,0:T(8,128)(2,1)S(1)} copy(bf16[4,16,32,1536]{3,2,0,1:T(8,128)(2,1)} %bitcast.126) | data formatting | bytes 12582912 | tf_op jit(solution)/shard_map/transpose | solution.py:84
  112.0 1.6 slice.114
  113.6 1.6 copy-done
  115.3 0.2 slice_bitcast_fusion.4
  115.5 3.0 %copy.42 = bf16[768,2048]{1,0:T(8,128)(2,1)} copy(bf16[768,2048]{0,1:T(8,128)(2,1)S(1)} %slice_bitcast_fusion.4) | data formatting | bytes 6291456 | tf_op jit(solution)/shard_map/dot_general | solution.py:90
  118.4 5.6 %fusion.80 = f32[768,3,4,64]{0,3,2,1:T(8,128)S(1)} fusion(bf16[768,2048,1,1]{0,1,3,2:T(8,128)(2,1)} %bitcast.127, bf16[3,4,64,2048]{3,2,1,0:T(8,128)(2,1)} %bitcast.128), kind=kOutput, calls=%fused_computation.115 | convolution fusion | flops 2415919104 | bytes 8650752 | tf_op jit(solution)/shard_map/dot_general | solution.py:90
  124.2 1.2 copy-done.2
  125.5 0.8 slice_negate_fusion
  126.3 1.0 constant_dynamic-slice_fusion.2
  127.5 1.0 fusion.64
  128.5 0.6 multiply_reduce_fusion
  129.1 1.0 fusion.62
  130.1 1.8 fusion.28
  132.0 2.3 %fusion.32 = f32[4,768]{1,0:T(4,128)S(1)} fusion(f32[4,768,768]{1,2,0:T(8,128)S(1)} %get-tuple-element.355, f32[4,768]{1,0:T(4,128)S(1)} %get-tuple-element.348, pred[768,768]{0,1:T(8,128)(4,1)S(1)} %copy-done.1), kind=kLoop, calls=%fused_computation.41 | loop fusion | flops 11793408 | bytes 10051584 | tf_op jit(solution)/shard_map/reduce_sum | solution.py:34
  134.3 3.9 %fusion.57 = f32[768,4,64]{0,2,1:T(8,128)S(1)} fusion(f32[4,768,768]{1,2,0:T(8,128)S(1)} %get-tuple-element.355, f32[4,768]{1,0:T(4,128)S(1)} %get-tuple-element.348, pred[768,768]{0,1:T(8,128)(4,1)S(1)} %copy-done.1, f32[768,4]{0,1:T(4,128)S(1)} %get-tuple-element.347, f32[768,4]{0,1:T(4,128)S(1)} %get-tuple-element.346, f32[768,3,4,64]{0,3,2,1:T(8,128)} %copy-done.2), kind=kOutput, calls=%fused_computation.60 | convolution fusion | flops 314179584 | bytes 11243520 | tf_op jit(solution)/shard_map/hqk,khd->qhd/dot_general | solution.py:35
  138.3 0.5 fusion.40
  138.8 0.7 fusion.51
  139.5 43.8 %while.21 = (s32[]{:T(128)}, f32[4,768]{1,0:T(4,128)S(1)}, f32[4,768]{1,0:T(4,128)S(1)}, f32[768,4,64]{0,2,1:T(8,128)S(1)}, s32[24]{0:T(128)S(1)}, /*index=5*/s3...) while((s32[]{:T(128)}, f32[4,768]{1,0:T(4,128)S(1)}, ...), condition=%wide.region_10.11_spmd.clone, body=%wide.region_7.10_spmd.clone.sunk | while | flops 846611456 | bytes 47256848 | solution.py:146
  139.8 0.7 fusion.93
  140.6 1.9 constant_dynamic-slice_fusion.4
  142.5 1.5 copy.59
  144.0 0.5 reshape.194
  144.5 2.7 %bitcast_reduce_fusion.2 = (f32[4,768]{1,0:T(4,128)S(1)}, f32[4,1024,768]{2,1,0:T(8,128)S(1)}) fusion(pred[1024]{0:T(1024)(128)(4,1)S(1)} %fusion.93, bf16[768,4,64]{0,2,1:T(8,128)(2,1)S(1)} %get-tuple-element.450, bf16[1024,2,4,64]{0,3,2,1:T(8,128)(2,1)S(1)} %reshape.194), kind=kOutput, calls=%fused_computation.4.clone.1 | convolution fusion | flops 412087296 | bytes 13513728 | tf_op jit(solution)/shard_map/while/body/eval_jaxpr/qhd,khd->hqk/dot_general | solution.py:29
  147.2 3.0 %fusion.96 = f32[768,4,64]{0,2,1:T(8,128)S(1)} fusion(f32[4,1024,768]{2,1,0:T(8,128)S(1)} %get-tuple-element.417, f32[4,768]{1,0:T(4,128)S(1)} %get-tuple-element.444, pred[1024]{0:T(1024)(128)(4,1)S(1)} %fusion.93, f32[768,4,64]{0,2,1:T(8,128)S(1)} %get-tuple-element.434, bf16[1024,2,4,64]{0,3,2,1:T(8,128)(2,1)S(1)} %reshape.194, ...), kind=kOutput, calls=%fused_computation.14.clone.1 | convolution fusion | flops 418775040 | bytes 14706688 | tf_op jit(solution)/shard_map/while/body/eval_jaxpr/hqk,khd->qhd/dot_general | solution.py:35
  150.2 4.0 %fusion.95 = f32[4,768]{1,0:T(4,128)S(1)} fusion(f32[4,1024,768]{2,1,0:T(8,128)S(1)} %get-tuple-element.417, f32[4,768]{1,0:T(4,128)S(1)} %get-tuple-element.444, pred[1024]{0:T(1024)(128)(4,1)S(1)} %fusion.93), kind=kLoop, calls=%fused_computation.9.clone.1 | loop fusion | flops 15725568 | bytes 12608512 | tf_op jit(solution)/shard_map/while/body/eval_jaxpr/reduce_sum | solution.py:34
  154.4 0.7 fusion.93
  155.1 1.9 constant_dynamic-slice_fusion.4
  157.0 1.5 copy.59
  158.5 0.5 reshape.194
  159.0 2.7 %bitcast_reduce_fusion.2 = (f32[4,768]{1,0:T(4,128)S(1)}, f32[4,1024,768]{2,1,0:T(8,128)S(1)}) fusion(pred[1024]{0:T(1024)(128)(4,1)S(1)} %fusion.93, bf16[768,4,64]{0,2,1:T(8,128)(2,1)S(1)} %get-tuple-element.450, bf16[1024,2,4,64]{0,3,2,1:T(8,128)(2,1)S(1)} %reshape.194), kind=kOutput, calls=%fused_computation.4.clone.1 | convolution fusion | flops 412087296 | bytes 13513728 | tf_op jit(solution)/shard_map/while/body/eval_jaxpr/qhd,khd->hqk/dot_general | solution.py:29
  161.7 3.0 %fusion.96 = f32[768,4,64]{0,2,1:T(8,128)S(1)} fusion(f32[4,1024,768]{2,1,0:T(8,128)S(1)} %get-tuple-element.417, f32[4,768]{1,0:T(4,128)S(1)} %get-tuple-element.444, pred[1024]{0:T(1024)(128)(4,1)S(1)} %fusion.93, f32[768,4,64]{0,2,1:T(8,128)S(1)} %get-tuple-element.434, bf16[1024,2,4,64]{0,3,2,1:T(8,128)(2,1)S(1)} %reshape.194, ...), kind=kOutput, calls=%fused_computation.14.clone.1 | convolution fusion | flops 418775040 | bytes 14706688 | tf_op jit(solution)/shard_map/while/body/eval_jaxpr/hqk,khd->qhd/dot_general | solution.py:35
  164.7 4.0 %fusion.95 = f32[4,768]{1,0:T(4,128)S(1)} fusion(f32[4,1024,768]{2,1,0:T(8,128)S(1)} %get-tuple-element.417, f32[4,768]{1,0:T(4,128)S(1)} %get-tuple-element.444, pred[1024]{0:T(1024)(128)(4,1)S(1)} %fusion.93), kind=kLoop, calls=%fused_computation.9.clone.1 | loop fusion | flops 15725568 | bytes 12608512 | tf_op jit(solution)/shard_map/while/body/eval_jaxpr/reduce_sum | solution.py:34
  168.9 0.7 fusion.93
  169.6 1.9 constant_dynamic-slice_fusion.4
  171.5 1.5 copy.59
  173.0 0.5 reshape.194
  173.5 2.7 %bitcast_reduce_fusion.2 = (f32[4,768]{1,0:T(4,128)S(1)}, f32[4,1024,768]{2,1,0:T(8,128)S(1)}) fusion(pred[1024]{0:T(1024)(128)(4,1)S(1)} %fusion.93, bf16[768,4,64]{0,2,1:T(8,128)(2,1)S(1)} %get-tuple-element.450, bf16[1024,2,4,64]{0,3,2,1:T(8,128)(2,1)S(1)} %reshape.194), kind=kOutput, calls=%fused_computation.4.clone.1 | convolution fusion | flops 412087296 | bytes 13513728 | tf_op jit(solution)/shard_map/while/body/eval_jaxpr/qhd,khd->hqk/dot_general | solution.py:29
  176.2 3.0 %fusion.96 = f32[768,4,64]{0,2,1:T(8,128)S(1)} fusion(f32[4,1024,768]{2,1,0:T(8,128)S(1)} %get-tuple-element.417, f32[4,768]{1,0:T(4,128)S(1)} %get-tuple-element.444, pred[1024]{0:T(1024)(128)(4,1)S(1)} %fusion.93, f32[768,4,64]{0,2,1:T(8,128)S(1)} %get-tuple-element.434, bf16[1024,2,4,64]{0,3,2,1:T(8,128)(2,1)S(1)} %reshape.194, ...), kind=kOutput, calls=%fused_computation.14.clone.1 | convolution fusion | flops 418775040 | bytes 14706688 | tf_op jit(solution)/shard_map/while/body/eval_jaxpr/hqk,khd->qhd/dot_general | solution.py:35
  179.3 4.0 %fusion.95 = f32[4,768]{1,0:T(4,128)S(1)} fusion(f32[4,1024,768]{2,1,0:T(8,128)S(1)} %get-tuple-element.417, f32[4,768]{1,0:T(4,128)S(1)} %get-tuple-element.444, pred[1024]{0:T(1024)(128)(4,1)S(1)} %fusion.93), kind=kLoop, calls=%fused_computation.9.clone.1 | loop fusion | flops 15725568 | bytes 12608512 | tf_op jit(solution)/shard_map/while/body/eval_jaxpr/reduce_sum | solution.py:34
  183.3 0.8 divide_convert_fusion
  184.1 1.2 slice.144
  185.3 0.6 copy.49
  186.0 1.0 maximum_convert_fusion
  187.0 0.6 copy.48
  187.6 2.7 %pad_maximum_fusion = bf16[768,2,256]{2,1,0:T(2,128)(2,1)} fusion(bf16[768,1,256]{2,1,0:T(2,128)(2,1)S(1)} %copy.49, bf16[768,1,256]{2,1,0:T(2,128)(2,1)S(1)} %copy.48), kind=kLoop, calls=%fused_computation.67 | loop fusion | flops 1572864 | bytes 1572864 | tf_op jit(solution)/shard_map/stack | solution.py:102
  190.3 29.6 %all-gather.4.cloned.1.call-done = bf16[768,2048]{0,1:T(8,128)(2,1)} async-done(((bf16[768,256]{0,1:T(8,128)(2,1)}), bf16[768,2048]{0,1:T(8,128)(2,1)}) %all-gather.4.cloned.1.call-update) | async-done | bytes 3145744 | tf_op jit(solution)/shard_map/all_gather | solution.py:152
  219.8 3.9 %convolution_convert_fusion = bf16[768,256]{1,0:T(8,128)(2,1)} fusion(bf16[768,2048]{0,1:T(8,128)(2,1)} %all-gather.4.cloned.1.call-done, bf16[2048,1536]{1,0:T(8,128)(2,1)} %bitcast.125), kind=kOutput, calls=%fused_computation.61 | convolution fusion | flops 805502976 | bytes 4587520 | tf_op jit(solution)/shard_map/dot_general | solution.py:154
  (50 shorter events, 1.0 us)
Async XLA Ops:
  7.2 27.6 %copy-start.7 = (s32[16]{0:T(128)S(1)}, s32[16]{0:T(128)}, u32[]{:S(2)}) copy-start(s32[16]{0:T(128)} %param.21) | copy-start | bytes 196
  7.2 30.2 %copy-start.6 = (f32[2048]{0:T(1024)S(1)}, f32[2048]{0:T(1024)}, u32[]{:S(2)}) copy-start(f32[2048]{0:T(1024)} %param.13) | copy-start | bytes 24580
  7.2 30.2 %copy-start.8 = (s32[1,24]{1,0:T(1,128)S(1)}, s32[1,24]{1,0:T(1,128)}, u32[]{:S(2)}) copy-start(s32[1,24]{1,0:T(1,128)} %param.18) | copy-start | bytes 292
  7.2 101.3 %all-gather.6.cloned.1.call-start = ((), (), s32[]{:S(2)}) async-start(), calls=%async_computation.3 | async-start | bytes 6684672 | tf_op jit(solution)/shard_map/all_gather | solution.py:83
  23.4 48.2 %all-to-all-start = ((bf16[8,768,256]{2,1,0:T(8,128)(2,1)}), bf16[8,768,256]{2,1,0:T(8,128)(2,1)}, u32[]{:S(2)}, u32[]{:S(2)}) async-start(bf16[8,768,256]{2,1,0:T(8,128)(2,1)} %broadcast_in_dim.157), calls=%async_computation | async-start | bytes 6291456 | tf_op jit(solution)/shard_map/all_to_all | solution.py:45
  34.1 185.8 %all-gather.4.cloned.1.call-start = ((), (), s32[]{:S(2)}) async-start(), calls=%async_computation.2 | async-start | bytes 3538944 | tf_op jit(solution)/shard_map/all_gather | solution.py:152
  112.0 3.3 %copy-start = (bf16[4,16,32,1536]{3,2,1,0:T(8,128)(2,1)}, bf16[4,16,32,1536]{3,2,1,0:T(8,128)(2,1)S(1)}, u32[]{:S(2)}) copy-start(bf16[4,16,32,1536]{3,2,1,0:T(8,128)(2,1)S(1)} %copy.41) | copy-start | bytes 18874372
  124.0 1.4 copy-start.2
  124.0 6.0 %copy-start.1 = (pred[768,768]{0,1:T(8,128)(4,1)S(1)}, pred[768,768]{0,1:T(8,128)(4,1)}, u32[]{:S(2)}) copy-start(pred[768,768]{0,1:T(8,128)(4,1)} %iota_compare_fusion) | copy-start | bytes 1769476
  125.5 6.4 %copy-start.3 = (bf16[768,4,48]{0,2,1:T(8,128)(2,1)}, bf16[768,4,48]{0,2,1:T(8,128)(2,1)S(1)}, u32[]{:S(2)}) copy-start(bf16[768,4,48]{0,2,1:T(8,128)(2,1)S(1)} %slice.113) | copy-start | bytes 884740
  130.1 4.2 %copy-start.4 = (bf16[768,4,16]{0,2,1:T(8,128)(2,1)}, bf16[768,4,16]{0,2,1:T(8,128)(2,1)S(1)}, u32[]{:S(2)}) copy-start(bf16[768,4,16]{0,2,1:T(8,128)(2,1)S(1)} %fusion.62) | copy-start | bytes 294916
  139.5 46.4 %copy-start.5 = (bf16[768,4,16]{0,2,1:T(8,128)(2,1)S(1)}, bf16[768,4,16]{0,2,1:T(8,128)(2,1)}, u32[]{:S(2)}) copy-start(bf16[768,4,16]{0,2,1:T(8,128)(2,1)} %copy-done.4) | copy-start | bytes 294916
Sparse Core Ops, SparseCore 0:
  20.7 87.7 all-gather.5
  184.3 35.5 all-gather.3
where the time goes:
time: 232 us; the launch traced here: 231 us
  waiting for transfers between devices  90.9 us (39%)
  local copies, waits for them, and re-layouts  35.6 us (15%)
  matrix products  33.6 us (14%)
  other arithmetic  31.3 us (13%)
  between operations  17 us (7%)
  blocking collectives  11 us (5%)
  starting transfers between devices  10.7 us (5%)
    all_to_all x1, waiting for transfers between devices, gather_columns(): received = lax.all_to_all(copies, 'narrow', 0, 0, tiled=False)  31.7 us
    all_gather x1, waiting for transfers between devices, local(): by_xz = lax.all_gather(by_x, 'wz', axis=0, tiled=False)  29.6 us
    all_gather x1, waiting for transfers between devices, local(): all_heads = lax.all_gather(head_values, 'narrow', axis=1, tiled=True)  29.6 us
    reduce_sum x5, other arithmetic, attend(): weight_sum = weight_sum * factor + jnp.sum(expo, axis=2)  14.9 us
    dot_general x5, matrix products, attend(): jnp.einsum('hqk,khd->qhd', expo.astype(jnp.bfloat16), values, preferred_e...  13.7 us
    all_to_all x1, blocking collectives, local(): lax.all_to_all(jnp.broadcast_to(merged[None], (along_x,) + merged.shape),...  11 us
    all_to_all x1, starting transfers between devices, gather_columns(): received = lax.all_to_all(copies, 'narrow', 0, 0, tiled=False)  10.7 us
    dot_general x5, matrix products, attend(): jnp.einsum('qhd,khd->hqk', queries, keys, preferred_element_type=jnp.floa...  10.4 us
  transfers between devices with their start and end apart: 3, of which 3 were waited for; matrix products, arithmetic and copies ran while one was open for 8% of the time, Pallas kernels for 0%

commit v1 on v0

--- a/solution.py
+++ b/solution.py
@@ -149,7 +149,9 @@
         .astype(jnp.bfloat16)
         .reshape(span_rows, local_width)
     )
-    all_heads = lax.all_gather(head_values, "narrow", axis=1, tiled=True)
+    all_heads = jnp.concatenate(
+        lax.all_to_all(jnp.stack(lax.axis_size("narrow") * [head_values]), "narrow", 0, 0), axis=1
+    )
     columns = all_heads
     branch_out = jnp.dot(columns, out_rows, preferred_element_type=jnp.float32)
     return (branch_out.astype(jnp.bfloat16), new_pages)

time: 232 us -> 242 us (1.043)
  starting transfers between devices: 10.7 us -> 18.9 us
  local copies, waits for them, and re-layouts: 35.6 us -> 39.8 us
    all_gather x1 -> x0, waiting for transfers between devices: 29.6 us -> none  [local(): all_heads = lax.all_gather(head_values, 'narrow', axis=1, tiled=True)]
    all_to_all x0 -> x1, waiting for transfers between devices: none -> 27.8 us  [local(): lax.all_to_all(jnp.stack(lax.axis_size('narrow') * [head_values]), 'narro...]
    all_to_all x0 -> x1, starting transfers between devices: none -> 8.21 us  [local(): lax.all_to_all(jnp.stack(lax.axis_size('narrow') * [head_values]), 'narro...]
  transfers between devices with their start and end apart: 3 -> 3, of which waited for: 3 -> 3; matrix products, arithmetic and copies ran while one was open for 8% -> 9% of each run, Pallas kernels for 0% -> 0%
where the time goes in v1:
time: 242 us; the launch traced here: 241 us
  waiting for transfers between devices  89.2 us (37%)
  local copies, waits for them, and re-layouts  39.8 us (16%)
  matrix products  32.7 us (14%)
  other arithmetic  31.8 us (13%)
  starting transfers between devices  18.9 us (8%)
  between operations  17 us (7%)
  blocking collectives  11 us (5%)
    all_to_all x1, waiting for transfers between devices, gather_columns(): received = lax.all_to_all(copies, 'narrow', 0, 0, tiled=False)  31.7 us
    all_gather x1, waiting for transfers between devices, local(): by_xz = lax.all_gather(by_x, 'wz', axis=0, tiled=False)  29.6 us
    all_to_all x1, waiting for transfers between devices, local(): lax.all_to_all(jnp.stack(lax.axis_size('narrow') * [head_values]), 'narro...  27.8 us
    reduce_sum x5, other arithmetic, attend(): weight_sum = weight_sum * factor + jnp.sum(expo, axis=2)  14.9 us
    dot_general x5, matrix products, attend(): jnp.einsum('hqk,khd->qhd', expo.astype(jnp.bfloat16), values, preferred_e...  13.7 us
    all_to_all x1, blocking collectives, local(): lax.all_to_all(jnp.broadcast_to(merged[None], (along_x,) + merged.shape),...  11 us
    all_to_all x1, starting transfers between devices, gather_columns(): received = lax.all_to_all(copies, 'narrow', 0, 0, tiled=False)  10.7 us
    dot_general x5, matrix products, attend(): jnp.einsum('qhd,khd->hqk', queries, keys, preferred_element_type=jnp.floa...  10.4 us
  transfers between devices with their start and end apart: 3, of which 3 were waited for; matrix products, arithmetic and copies ran while one was open for 9% of the time, Pallas kernels for 0%

profile of v1, /device:TPU:1, one launch (start us, length us, event | category | flops | bytes accessed | tf_op | source)
XLA Modules:
  0.0 240.8 jit_solution(1803324508484641983)
XLA Ops:
  7.2 0.8 copy.58
  8.0 0.8 copy.57
  8.8 0.7 pad_maximum_fusion.3
  9.6 11.0 %all_to_all.15 = bf16[4,32,1536]{2,1,0:T(8,128)(2,1)} all-to-all(bf16[4,32,1536]{2,1,0:T(8,128)(2,1)S(1)} %broadcast_in_dim.158), channel_id=1, replica_groups=mesh['wx'=4,'wz'=16,'narrow'=8] {'wx'}, dimensions={0} | all-to-all | bytes 786432 | tf_op jit(solution)/shard_map/all_to_all | solution.py:80
  20.6 2.8 %broadcast_in_dim.157 = bf16[8,768,256]{2,1,0:T(8,128)(2,1)} broadcast(bf16[768,256]{1,0:T(8,128)(2,1)} %param.12), dimensions={1,2} | broadcast | bytes 3538944 | tf_op jit(solution)/shard_map/broadcast_in_dim | solution.py:44
  23.4 10.7 %all-to-all-start = ((bf16[8,768,256]{2,1,0:T(8,128)(2,1)}), bf16[8,768,256]{2,1,0:T(8,128)(2,1)}, u32[]{:S(2)}, u32[]{:S(2)}) async-start(bf16[8,768,256]{2,1,0:T(8,128)(2,1)} %broadcast_in_dim.157), calls=%async_computation | async-start | bytes 6291456 | tf_op jit(solution)/shard_map/all_to_all | solution.py:45
  34.8 0.6 fusion.78
  37.4 0.6 scatter_custom_fusion
  38.2 0.6 pad_maximum_fusion.4
  38.9 1.0 iota_compare_fusion
  39.9 31.7 %all-to-all-done = bf16[8,768,256]{2,1,0:T(8,128)(2,1)} async-done(((bf16[8,768,256]{2,1,0:T(8,128)(2,1)}), bf16[8,768,256]{2,1,0:T(8,128)(2,1)}, u32[]{:S(2)}, u32[]{:S(2)}) %all-to-all-start) | async-done | bytes 3145760 | tf_op jit(solution)/shard_map/all_to_all | solution.py:45
  71.6 3.2 %copy.40 = bf16[8,768,256]{1,2,0:T(8,128)(2,1)S(1)} copy(bf16[8,768,256]{2,1,0:T(8,128)(2,1)} %all-to-all-done) | data formatting | bytes 6291456 | tf_op jit(solution)/shard_map/all_to_all | solution.py:45
  74.8 0.5 convert_reduce_fusion
  75.3 0.9 fusion.33
  76.2 2.6 %fusion.35 = bf16[8,768,256]{1,2,0:T(8,128)(2,1)} fusion(bf16[8,768,256]{1,2,0:T(8,128)(2,1)S(1)} %copy.40, f32[8,256]{1,0:T(8,128)S(1)} %mul.207, f32[768]{0:T(1024)S(1)} %add_rsqrt_fusion, f32[768]{0:T(1024)S(1)} %broadcast_multiply_fusion), kind=kLoop, calls=%fused_computation.44 | loop fusion | flops 7864320 | bytes 6305792 | tf_op jit(solution)/shard_map/convert.3
  78.9 29.6 %all-gather.3.cloned.1.call-done = bf16[64,32,1536]{2,1,0:T(8,128)(2,1)} async-done(((bf16[4,32,1536]{2,1,0:T(8,128)(2,1)}), bf16[64,32,1536]{2,1,0:T(8,128)(2,1)}) %all-gather.3.cloned.1.call-update) | async-done | bytes 6291472 | tf_op jit(solution)/shard_map/all_gather | solution.py:83
  108.5 3.5 %copy.42 = bf16[4,16,32,1536]{3,2,1,0:T(8,128)(2,1)S(1)} copy(bf16[4,16,32,1536]{3,2,0,1:T(8,128)(2,1)} %bitcast.129) | data formatting | bytes 12582912 | tf_op jit(solution)/shard_map/transpose | solution.py:84
  112.0 1.6 slice.114
  113.6 1.7 copy-done
  115.3 0.2 slice_bitcast_fusion.4
  115.5 3.0 %copy.43 = bf16[768,2048]{1,0:T(8,128)(2,1)} copy(bf16[768,2048]{0,1:T(8,128)(2,1)S(1)} %slice_bitcast_fusion.4) | data formatting | bytes 6291456 | tf_op jit(solution)/shard_map/dot_general | solution.py:90
  118.4 5.6 %fusion.80 = f32[768,3,4,64]{0,3,2,1:T(8,128)S(1)} fusion(bf16[768,2048,1,1]{0,1,3,2:T(8,128)(2,1)} %bitcast.131, bf16[3,4,64,2048]{3,2,1,0:T(8,128)(2,1)} %bitcast.132), kind=kOutput, calls=%fused_computation.115 | convolution fusion | flops 2415919104 | bytes 8650752 | tf_op jit(solution)/shard_map/dot_general | solution.py:90
  124.2 1.3 copy-done.2
  125.5 0.8 slice_negate_fusion
  126.3 1.0 constant_dynamic-slice_fusion.2
  127.5 1.0 fusion.64
  128.5 0.6 multiply_reduce_fusion
  129.1 1.0 fusion.62
  130.1 1.8 fusion.28
  132.0 2.3 fusion.32
  134.3 3.9 %fusion.57 = f32[768,4,64]{0,2,1:T(8,128)S(1)} fusion(f32[4,768,768]{1,2,0:T(8,128)S(1)} %get-tuple-element.355, f32[4,768]{1,0:T(4,128)S(1)} %get-tuple-element.348, pred[768,768]{0,1:T(8,128)(4,1)S(1)} %copy-done.1, f32[768,4]{0,1:T(4,128)S(1)} %get-tuple-element.347, f32[768,4]{0,1:T(4,128)S(1)} %get-tuple-element.346, f32[768,3,4,64]{0,3,2,1:T(8,128)} %copy-done.2), kind=kOutput, calls=%fused_computation.60 | convolution fusion | flops 314179584 | bytes 11243520 | tf_op jit(solution)/shard_map/hqk,khd->qhd/dot_general | solution.py:35
  138.3 0.5 fusion.40
  138.8 0.7 fusion.51
  139.5 43.8 %while.21 = (s32[]{:T(128)}, f32[4,768]{1,0:T(4,128)S(1)}, f32[4,768]{1,0:T(4,128)S(1)}, f32[768,4,64]{0,2,1:T(8,128)S(1)}, s32[24]{0:T(128)S(1)}, /*index=5*/s3...) while((s32[]{:T(128)}, f32[4,768]{1,0:T(4,128)S(1)}, ...), condition=%wide.region_10.11_spmd.clone, body=%wide.region_7.10_spmd.clone.sunk | while | flops 846611456 | bytes 47256848 | solution.py:146
  139.8 0.7 fusion.93
  140.6 1.9 constant_dynamic-slice_fusion.4
  142.5 1.5 copy.60
  144.0 0.5 reshape.200
  144.5 2.7 %bitcast_reduce_fusion.2 = (f32[4,768]{1,0:T(4,128)S(1)}, f32[4,1024,768]{2,1,0:T(8,128)S(1)}) fusion(pred[1024]{0:T(1024)(128)(4,1)S(1)} %fusion.93, bf16[768,4,64]{0,2,1:T(8,128)(2,1)S(1)} %get-tuple-element.450, bf16[1024,2,4,64]{0,3,2,1:T(8,128)(2,1)S(1)} %reshape.200), kind=kOutput, calls=%fused_computation.4.clone.1 | convolution fusion | flops 412087296 | bytes 13513728 | tf_op jit(solution)/shard_map/while/body/eval_jaxpr/qhd,khd->hqk/dot_general | solution.py:29
  147.2 3.0 %fusion.96 = f32[768,4,64]{0,2,1:T(8,128)S(1)} fusion(f32[4,1024,768]{2,1,0:T(8,128)S(1)} %get-tuple-element.417, f32[4,768]{1,0:T(4,128)S(1)} %get-tuple-element.444, pred[1024]{0:T(1024)(128)(4,1)S(1)} %fusion.93, f32[768,4,64]{0,2,1:T(8,128)S(1)} %get-tuple-element.434, bf16[1024,2,4,64]{0,3,2,1:T(8,128)(2,1)S(1)} %reshape.200, ...), kind=kOutput, calls=%fused_computation.14.clone.1 | convolution fusion | flops 418775040 | bytes 14706688 | tf_op jit(solution)/shard_map/while/body/eval_jaxpr/hqk,khd->qhd/dot_general | solution.py:35
  150.2 4.0 %fusion.95 = f32[4,768]{1,0:T(4,128)S(1)} fusion(f32[4,1024,768]{2,1,0:T(8,128)S(1)} %get-tuple-element.417, f32[4,768]{1,0:T(4,128)S(1)} %get-tuple-element.444, pred[1024]{0:T(1024)(128)(4,1)S(1)} %fusion.93), kind=kLoop, calls=%fused_computation.9.clone.1 | loop fusion | flops 15725568 | bytes 12608512 | tf_op jit(solution)/shard_map/while/body/eval_jaxpr/reduce_sum | solution.py:34
  154.4 0.7 fusion.93
  155.1 1.9 constant_dynamic-slice_fusion.4
  157.0 1.5 copy.60
  158.5 0.5 reshape.200
  159.0 2.7 %bitcast_reduce_fusion.2 = (f32[4,768]{1,0:T(4,128)S(1)}, f32[4,1024,768]{2,1,0:T(8,128)S(1)}) fusion(pred[1024]{0:T(1024)(128)(4,1)S(1)} %fusion.93, bf16[768,4,64]{0,2,1:T(8,128)(2,1)S(1)} %get-tuple-element.450, bf16[1024,2,4,64]{0,3,2,1:T(8,128)(2,1)S(1)} %reshape.200), kind=kOutput, calls=%fused_computation.4.clone.1 | convolution fusion | flops 412087296 | bytes 13513728 | tf_op jit(solution)/shard_map/while/body/eval_jaxpr/qhd,khd->hqk/dot_general | solution.py:29
  161.7 3.0 %fusion.96 = f32[768,4,64]{0,2,1:T(8,128)S(1)} fusion(f32[4,1024,768]{2,1,0:T(8,128)S(1)} %get-tuple-element.417, f32[4,768]{1,0:T(4,128)S(1)} %get-tuple-element.444, pred[1024]{0:T(1024)(128)(4,1)S(1)} %fusion.93, f32[768,4,64]{0,2,1:T(8,128)S(1)} %get-tuple-element.434, bf16[1024,2,4,64]{0,3,2,1:T(8,128)(2,1)S(1)} %reshape.200, ...), kind=kOutput, calls=%fused_computation.14.clone.1 | convolution fusion | flops 418775040 | bytes 14706688 | tf_op jit(solution)/shard_map/while/body/eval_jaxpr/hqk,khd->qhd/dot_general | solution.py:35
  164.7 4.0 %fusion.95 = f32[4,768]{1,0:T(4,128)S(1)} fusion(f32[4,1024,768]{2,1,0:T(8,128)S(1)} %get-tuple-element.417, f32[4,768]{1,0:T(4,128)S(1)} %get-tuple-element.444, pred[1024]{0:T(1024)(128)(4,1)S(1)} %fusion.93), kind=kLoop, calls=%fused_computation.9.clone.1 | loop fusion | flops 15725568 | bytes 12608512 | tf_op jit(solution)/shard_map/while/body/eval_jaxpr/reduce_sum | solution.py:34
  168.9 0.7 fusion.93
  169.6 1.9 constant_dynamic-slice_fusion.4
  171.6 1.5 copy.60
  173.0 0.5 reshape.200
  173.5 2.7 %bitcast_reduce_fusion.2 = (f32[4,768]{1,0:T(4,128)S(1)}, f32[4,1024,768]{2,1,0:T(8,128)S(1)}) fusion(pred[1024]{0:T(1024)(128)(4,1)S(1)} %fusion.93, bf16[768,4,64]{0,2,1:T(8,128)(2,1)S(1)} %get-tuple-element.450, bf16[1024,2,4,64]{0,3,2,1:T(8,128)(2,1)S(1)} %reshape.200), kind=kOutput, calls=%fused_computation.4.clone.1 | convolution fusion | flops 412087296 | bytes 13513728 | tf_op jit(solution)/shard_map/while/body/eval_jaxpr/qhd,khd->hqk/dot_general | solution.py:29
  176.2 3.0 %fusion.96 = f32[768,4,64]{0,2,1:T(8,128)S(1)} fusion(f32[4,1024,768]{2,1,0:T(8,128)S(1)} %get-tuple-element.417, f32[4,768]{1,0:T(4,128)S(1)} %get-tuple-element.444, pred[1024]{0:T(1024)(128)(4,1)S(1)} %fusion.93, f32[768,4,64]{0,2,1:T(8,128)S(1)} %get-tuple-element.434, bf16[1024,2,4,64]{0,3,2,1:T(8,128)(2,1)S(1)} %reshape.200, ...), kind=kOutput, calls=%fused_computation.14.clone.1 | convolution fusion | flops 418775040 | bytes 14706688 | tf_op jit(solution)/shard_map/while/body/eval_jaxpr/hqk,khd->qhd/dot_general | solution.py:35
  179.3 4.0 %fusion.95 = f32[4,768]{1,0:T(4,128)S(1)} fusion(f32[4,1024,768]{2,1,0:T(8,128)S(1)} %get-tuple-element.417, f32[4,768]{1,0:T(4,128)S(1)} %get-tuple-element.444, pred[1024]{0:T(1024)(128)(4,1)S(1)} %fusion.93), kind=kLoop, calls=%fused_computation.9.clone.1 | loop fusion | flops 15725568 | bytes 12608512 | tf_op jit(solution)/shard_map/while/body/eval_jaxpr/reduce_sum | solution.py:34
  183.4 1.9 stack.6
  185.3 8.2 %all-to-all-start.2 = ((bf16[8,768,256]{1,2,0:T(8,128)(2,1)}), bf16[8,768,256]{1,2,0:T(8,128)(2,1)S(1)}, u32[]{:S(2)}, u32[]{:S(2)}) async-start(bf16[8,768,256]{1,2,0:T(8,128)(2,1)} %stack.6), calls=%async_computation.2 | async-start | bytes 6291456 | tf_op jit(solution)/shard_map/all_to_all | solution.py:153
  193.5 1.2 slice.144
  194.7 1.8 copy.50
  196.5 1.0 maximum_convert_fusion
  197.5 1.8 copy.49
  199.2 3.9 %pad_maximum_fusion = bf16[768,2,256]{2,1,0:T(2,128)(2,1)} fusion(bf16[768,1,256]{2,1,0:T(2,128)(2,1)} %copy.50, bf16[768,1,256]{2,1,0:T(2,128)(2,1)} %copy.49), kind=kLoop, calls=%fused_computation.67 | loop fusion | flops 1572864 | bytes 1572864 | tf_op jit(solution)/shard_map/stack | solution.py:102
  203.1 27.8 %all-to-all-done.2 = bf16[8,768,256]{1,2,0:T(8,128)(2,1)S(1)} async-done(((bf16[8,768,256]{1,2,0:T(8,128)(2,1)}), bf16[8,768,256]{1,2,0:T(8,128)(2,1)S(1)}, u32[]{:S(2)}, u32[]{:S(2)}) %all-to-all-start.2) | async-done | bytes 3145760 | tf_op jit(solution)/shard_map/all_to_all | solution.py:153
  230.9 3.0 %convolution_convert_fusion = bf16[768,256]{1,0:T(8,128)(2,1)} fusion(bf16[768,2048]{0,1:T(8,128)(2,1)S(1)} %bitcast.130, bf16[2048,1536]{1,0:T(8,128)(2,1)} %bitcast.128), kind=kOutput, calls=%fused_computation.61 | convolution fusion | flops 805502976 | bytes 4587520 | tf_op jit(solution)/shard_map/dot_general | solution.py:156
  (48 shorter events, 1.2 us)
Async XLA Ops:
  7.2 27.5 %copy-start.6 = (s32[16]{0:T(128)S(1)}, s32[16]{0:T(128)}, u32[]{:S(2)}) copy-start(s32[16]{0:T(128)} %param.21) | copy-start | bytes 196
  7.2 30.2 %copy-start.5 = (f32[2048]{0:T(1024)S(1)}, f32[2048]{0:T(1024)}, u32[]{:S(2)}) copy-start(f32[2048]{0:T(1024)} %param.13) | copy-start | bytes 24580
  7.2 30.2 %copy-start.7 = (s32[1,24]{1,0:T(1,128)S(1)}, s32[1,24]{1,0:T(1,128)}, u32[]{:S(2)}) copy-start(s32[1,24]{1,0:T(1,128)} %param.18) | copy-start | bytes 292
  7.2 101.3 %all-gather.3.cloned.1.call-start = ((), (), s32[]{:S(2)}) async-start(), calls=%async_computation.3 | async-start | bytes 6684672 | tf_op jit(solution)/shard_map/all_gather | solution.py:83
  23.4 48.2 %all-to-all-start = ((bf16[8,768,256]{2,1,0:T(8,128)(2,1)}), bf16[8,768,256]{2,1,0:T(8,128)(2,1)}, u32[]{:S(2)}, u32[]{:S(2)}) async-start(bf16[8,768,256]{2,1,0:T(8,128)(2,1)} %broadcast_in_dim.157), calls=%async_computation | async-start | bytes 6291456 | tf_op jit(solution)/shard_map/all_to_all | solution.py:45
  112.0 3.3 %copy-start = (bf16[4,16,32,1536]{3,2,1,0:T(8,128)(2,1)}, bf16[4,16,32,1536]{3,2,1,0:T(8,128)(2,1)S(1)}, u32[]{:S(2)}) copy-start(bf16[4,16,32,1536]{3,2,1,0:T(8,128)(2,1)S(1)} %copy.42) | copy-start | bytes 18874372
  124.0 1.4 copy-start.2
  124.0 6.1 %copy-start.1 = (pred[768,768]{0,1:T(8,128)(4,1)S(1)}, pred[768,768]{0,1:T(8,128)(4,1)}, u32[]{:S(2)}) copy-start(pred[768,768]{0,1:T(8,128)(4,1)} %iota_compare_fusion) | copy-start | bytes 1769476
  125.5 6.4 %copy-start.3 = (bf16[768,4,48]{0,2,1:T(8,128)(2,1)}, bf16[768,4,48]{0,2,1:T(8,128)(2,1)S(1)}, u32[]{:S(2)}) copy-start(bf16[768,4,48]{0,2,1:T(8,128)(2,1)S(1)} %slice.113) | copy-start | bytes 884740
  130.1 4.2 %copy-start.4 = (bf16[768,4,16]{0,2,1:T(8,128)(2,1)}, bf16[768,4,16]{0,2,1:T(8,128)(2,1)S(1)}, u32[]{:S(2)}) copy-start(bf16[768,4,16]{0,2,1:T(8,128)(2,1)S(1)} %fusion.62) | copy-start | bytes 294916
  185.3 45.6 %all-to-all-start.2 = ((bf16[8,768,256]{1,2,0:T(8,128)(2,1)}), bf16[8,768,256]{1,2,0:T(8,128)(2,1)S(1)}, u32[]{:S(2)}, u32[]{:S(2)}) async-start(bf16[8,768,256]{1,2,0:T(8,128)(2,1)} %stack.6), calls=%async_computation.2 | async-start | bytes 6291456 | tf_op jit(solution)/shard_map/all_to_all | solution.py:153
Sparse Core Ops, SparseCore 0:
  20.7 87.7 all-gather.2
